TPU v7x, 128 devices: a whole 4x4x4 slice. The times are simulated.
128 devices in a mesh: grp: 2 (over y_hi), row: 64 (over z, y_lo, x, core).
Axes of the slice: x: 4, y: 4 (y_hi: 2, y_lo: 2; y = y_hi * 2 + y_lo), z: 4, core: 2. Of those that a mesh axis runs over, the one named last changes fastest.
Arguments:
- features: bfloat16 [65536, 256], P(('grp', 'row')), may hold values from -6 to 6
- weight: bfloat16 [256, 256], replicated, may hold values from -0.375 to 0.375
- block_vals: bfloat16 [2, 512, 16, 128, 128], P('grp', 'row'), may hold values from -0.125 to 0.125
- block_cols: int32 [2, 512, 16], P('grp', 'row'), may hold values from 0 to 255, as said below
- block_count: int32 [2, 512], P('grp', 'row'), may hold values from 1 to 16, as said below
- cotangent: bfloat16 [65536, 256], P(('grp', 'row')), may hold values from -6 to 6
Outputs:
- activated: bfloat16 [65536, 256], P(('grp', 'row'))
- weight_grad: float32 [256, 256], replicated
- input_grad: bfloat16 [65536, 256], P(('grp', 'row'))
Inputs may be any that keep to these rules, and one draw needn't show every extreme that they name: `block_cols`: within one destination row block the 16 column blocks are distinct and ascending. `block_count`: in every draw some device holds 16 live slots in each of its row blocks.
All inputs are finite; a program needn't handle non-finite values.
Results may differ from a plain program's by a relative error of at most 0.0062.
Values may be sent and summed in bfloat16 or wider, within the bound.
No kernel may reach another device: no remote copies, remote signals or barrier semaphores. Data moves between devices by JAX's collectives and lax.ppermute only.
A program may use at most 128 MiB of HBM per device.

v0:
```python
import math
import jax
import jax.numpy as jnp
from jax import lax
from jax.sharding import PartitionSpec as P


def silu_slope(pre):
    sigma = jax.nn.sigmoid(pre)
    return sigma * (1.0 + pre * (1.0 - sigma))


def body(features, weight, block_vals, block_cols, block_count, cotangent):
    rows_dev, width = features.shape
    block = block_vals.shape[-1]
    slot_total = block_vals.shape[2]
    groups = lax.axis_size("grp")
    members = lax.axis_size("row")
    verts = rows_dev * groups * members
    slots = jnp.arange(slot_total)
    gathered = lax.all_gather(features, "row", axis=0, tiled=True)
    col_blocks = gathered.shape[0] // block
    panel_blocks = gathered.reshape(col_blocks, block, width)

    def aggregate(items):
        values, columns, count = items
        masked = jnp.where((slots < count)[:, None, None], values, jnp.zeros_like(values))
        picked = panel_blocks[columns]
        return jnp.einsum("kij,kjf->if", masked, picked, preferred_element_type=jnp.float32)

    partial_value = lax.map(aggregate, (block_vals[0], block_cols[0], block_count[0])).reshape(
        -1, width
    )
    summed = lax.psum_scatter(partial_value, "grp", scatter_dimension=0, tiled=True)
    aggregated = summed.astype(jnp.bfloat16)
    pre = jnp.dot(aggregated, weight, preferred_element_type=jnp.float32)
    activated = jax.nn.silu(pre).astype(jnp.bfloat16)
    pre_grad = (cotangent.astype(jnp.float32) * silu_slope(pre)).astype(jnp.bfloat16)
    local_grad = jnp.dot(aggregated.T, pre_grad, preferred_element_type=jnp.float32)
    own_grad = jnp.dot(pre_grad, weight.T, preferred_element_type=jnp.float32).astype(jnp.bfloat16)
    rows_grad = lax.all_gather(own_grad, "grp", axis=0, tiled=True)
    weight_grad = lax.psum(local_grad, ("grp", "row")) * (1.0 / math.sqrt(verts))
    by_block = rows_grad.reshape(-1, block, width)

    def spread(carry, items):
        values, columns, count, grad_block = items
        masked = jnp.where((slots < count)[:, None, None], values, jnp.zeros_like(values))
        contrib = jnp.einsum("kij,if->kjf", masked, grad_block, preferred_element_type=jnp.float32)
        return (carry.at[columns].add(contrib), None)

    total, unused = lax.scan(
        spread,
        jnp.zeros((col_blocks, block, width), jnp.float32),
        (block_vals[0], block_cols[0], block_count[0], by_block),
    )
    term = total.reshape(-1, width)
    input_grad = lax.psum_scatter(term, "row", scatter_dimension=0, tiled=True).astype(jnp.bfloat16)
    return (activated, weight_grad, input_grad)


def solution(mesh):
    placed = (
        P(("grp", "row"), None),
        P(),
        P("grp", "row", None, None, None),
        P("grp", "row", None),
        P("grp", "row"),
        P(("grp", "row"), None),
    )
    return jax.shard_map(
        body,
        mesh=mesh,
        in_specs=placed,
        out_specs=(P(("grp", "row"), None), P(), P(("grp", "row"), None)),
        check_vma=False,
    )
```

profile of v0, /device:TPU:0, one launch (start us, length us, event | category | flops | bytes accessed | tf_op | source)
XLA Modules:
  0.0 743.3 jit_solution(15940612499893916046)
XLA Ops:
  8.0 127.3 %all-gather.2.cloned.1.call-done = bf16[32768,256]{1,0:T(8,128)(2,1)} async-done(((bf16[512,256]{1,0:T(8,128)(2,1)}), bf16[32768,256]{1,0:T(8,128)(2,1)}) %all-gather.2.cloned.1.call-update) | async-done | bytes 16777232 | tf_op jit(solution)/shard_map/all_gather | solution.py:21
  135.3 88.4 %while.22 = (s32[]{:T(128)}, f32[8,128,256]{2,1,0:T(8,128)}, s32[8]{0:T(128)}, bf16[8,16,128,128]{3,2,1,0:T(8,128)(2,1)}, s32[8,16]{1,0:T(8,128)}, /*index=5*/bf16[256,128,256]{2,1,0:T(8,128)(2,1)}, s32[]{:T(128)}) while((s32[]{:T(128)}, f32[8,128,256]{2,1,0:T(8,128)}, s32[8]{0:T(128)}, bf16[8,16,128,128]{3,2,1,0:T(8,128)(2,1)}, ...), condition=%wide.region_1.2_spmd.clone, body=%wide.region_0.1_spmd.clone.sunk | while | flops 134480960 | bytes 3806601 | solution.py:31
  135.3 1.2 dynamic_slice.67
  137.9 6.4 gather_fusion
  144.3 2.1 fusion.42
  146.3 1.2 dynamic_slice.67
  148.9 6.4 gather_fusion
  155.3 2.1 fusion.42
  157.4 1.2 dynamic_slice.67
  160.0 6.4 gather_fusion
  166.4 2.1 fusion.42
  168.4 1.2 dynamic_slice.67
  171.0 6.4 gather_fusion
  177.4 2.1 fusion.42
  182.1 6.4 gather_fusion
  188.5 2.0 fusion.42
  193.1 6.4 gather_fusion
  199.5 2.1 fusion.42
  204.1 6.4 gather_fusion
  210.5 2.1 fusion.42
  215.2 6.4 gather_fusion
  221.6 2.1 fusion.42
  223.7 6.5 copy.9
  230.2 17.2 %reduce-scatter.3.cloned.1.call-done = f32[512,256]{1,0:T(8,128)} async-done(((f32[1024,256]{1,0:T(8,128)}), f32[512,256]{1,0:T(8,128)}) %reduce-scatter.3.cloned.1.call-update) | async-done | bytes 524304 | tf_op jit(solution)/shard_map/reduce_scatter | solution.py:34
  247.4 2.2 multiply_convert_fusion
  250.9 10.2 %all_gather.7 = bf16[1024,256]{1,0:T(8,128)(2,1)S(1)} all-gather(bf16[512,256]{1,0:T(8,128)(2,1)S(1)} %convolution_convert_fusion), channel_id=1, replica_groups=mesh['grp'=2,'row'=64] {'grp'}, dimensions={0}, use_global_device_ids=true | all-gather | bytes 786432 | tf_op jit(solution)/shard_map/all_gather | solution.py:41
  261.1 11.2 %broadcast_in_dim.28 = f32[256,128,256]{2,1,0:T(8,128)} broadcast(f32[]{:T(128)} %constant.27.clone.1), dimensions={} | broadcast | bytes 33554436 | tf_op jit(solution)/shard_map/broadcast_in_dim | solution.py:53
  272.4 63.8 %while.23 = (s32[]{:T(128)}, f32[256,128,256]{2,1,0:T(8,128)}, s32[8,16]{1,0:T(8,128)}, s32[8]{0:T(128)S(1)}, bf16[8,16,128,128]{2,3,1,0:T(8,128)(2,1)}, /*index=5*/bf16[8,128,256]{2,1,0:T(8,128)(2,1)S(1)}, s32[]{:T(128)}) while((s32[]{:T(128)}, f32[256,128,256]{2,1,0:T(8,128)}, s32[8,16]{1,0:T(8,128)}, s32[8]{0:T(128)S(1)}, ...), condition=%wide.region_6.7_spmd.clone, body=%wide.region_4.6_spmd.clone.sunk | while | flops 135004224 | bytes 8980281 | solution.py:51
  274.2 1.5 fusion.46
  275.7 4.6 scatter_fusion
  282.2 1.5 fusion.46
  283.7 4.6 scatter_fusion
  290.2 1.5 fusion.46
  291.7 4.6 scatter_fusion
  298.2 1.5 fusion.46
  299.7 4.6 scatter_fusion
  306.2 1.5 fusion.46
  307.7 4.6 scatter_fusion
  314.1 1.5 fusion.46
  315.7 4.6 scatter_fusion
  322.1 1.5 fusion.46
  323.6 4.6 scatter_fusion
  330.1 1.5 fusion.46
  331.6 4.6 scatter_fusion
  336.2 58.5 %all-reduce.2.cloned.1.call-done = f32[256,256]{1,0:T(8,128)} async-done(((f32[256,256]{1,0:T(8,128)}), f32[256,256]{1,0:T(8,128)}) %all-reduce.2.cloned.1.call-update) | async-done | bytes 262160 | tf_op jit(solution)/shard_map/psum | solution.py:42
  394.8 1.7 broadcast_multiply_fusion
  396.5 338.6 %reduce-scatter.5.cloned.1.call-done = f32[512,256]{1,0:T(8,128)} async-done(((f32[32768,256]{1,0:T(8,128)}), f32[512,256]{1,0:T(8,128)}) %reduce-scatter.5.cloned.1.call-update) | async-done | bytes 524304 | tf_op jit(solution)/shard_map/reduce_scatter | solution.py:57
  735.0 1.8 convert_element_type.23
  (71 shorter events, 32.6 us)
Async XLA Ops:
  7.2 240.2 %copy-start = (bf16[256,256]{1,0:T(8,128)(2,1)S(1)}, bf16[256,256]{1,0:T(8,128)(2,1)}, u32[]{:S(2)}) copy-start(bf16[256,256]{1,0:T(8,128)(2,1)} %param.11) | copy-start | bytes 393220
  7.2 128.1 %all-gather.2.cloned.1.call-start = ((), (), s32[]{:S(2)}) async-start(), calls=%async_computation.2 | async-start | bytes 17039360 | tf_op jit(solution)/shard_map/all_gather | solution.py:21
  7.9 239.5 %reduce-scatter.3.cloned.1.call-start = ((), (), s32[]{:S(2)}) async-start(), calls=%async_computation.3 | async-start | bytes 1572864 | tf_op jit(solution)/shard_map/reduce_scatter | solution.py:34
  223.7 23.7 %copy-start.2 = (bf16[512,256]{1,0:T(8,128)(2,1)S(1)}, bf16[512,256]{1,0:T(8,128)(2,1)}, u32[]{:S(2)}) copy-start(bf16[512,256]{1,0:T(8,128)(2,1)} %param.15) | copy-start | bytes 786436
  223.7 171.1 %all-reduce.2.cloned.1.call-start = ((), (), s32[]{:S(2)}) async-start(), calls=%async_computation.4 | async-start | bytes 524288 | tf_op jit(solution)/shard_map/psum | solution.py:42
  247.4 2.5 copy-start.1
  250.9 484.1 %reduce-scatter.5.cloned.1.call-start = ((), (), s32[]{:S(2)}) async-start(), calls=%async_computation.5 | async-start | bytes 34078720 | tf_op jit(solution)/shard_map/reduce_scatter | solution.py:57
  261.1 11.2 %copy-start.3 = (s32[8]{0:T(128)S(1)}, s32[8]{0:T(128)}, u32[]{:S(2)}) copy-start(s32[8]{0:T(128)} %get-tuple-element.273) | copy-start | bytes 100
Sparse Core Ops, SparseCore 0:
  9.7 125.4 all-gather.1
  223.8 23.5 reduce-scatter.2
  253.4 141.3 all-reduce.1
  397.2 337.8 reduce-scatter.4
where the time goes:
time: 746 us; the launch traced here: 743 us
  waiting for transfers between devices  542 us (73%)
  local copies, waits for them, and re-layouts  83.3 us (11%)
  other arithmetic  61.3 us (8%)
  matrix products  32 us (4%)
  between operations  13.8 us (2%)
  blocking collectives  10.2 us (1%)
    reduce_scatter x1, waiting for transfers between devices, body(): lax.psum_scatter(term, 'row', scatter_dimension=0, tiled=True)  339 us
    all_gather x1, waiting for transfers between devices, body(): gathered = lax.all_gather(features, 'row', axis=0, tiled=True)  127 us
    psum x1, waiting for transfers between devices, body(): lax.psum(local_grad, ('grp', 'row')) * (1.0 / math.sqrt(verts))  58.5 us
    gather x8, local copies, waits for them, and re-layouts, aggregate(): picked = panel_blocks[columns]  51.1 us
    scatter-add x8, other arithmetic, spread(): return (carry.at[columns].add(contrib), None)  36.9 us
    reduce_scatter x1, waiting for transfers between devices, body(): lax.psum_scatter(partial_value, 'grp', scatter_dimension=0, tiled=True)  17.2 us
    dot_general x8, matrix products, aggregate(): jnp.einsum('kij,kjf->if', masked, picked, preferred_element_type=jnp.floa...  16.4 us
  transfers between devices with their start and end apart: 4, of which 4 were waited for; matrix products, arithmetic and copies ran while one was open for 11% of the time, Pallas kernels for 0%

commit v1 on v0

--- a/solution.py
+++ b/solution.py
@@ -39,7 +39,7 @@
     local_grad = jnp.dot(aggregated.T, pre_grad, preferred_element_type=jnp.float32)
     own_grad = jnp.dot(pre_grad, weight.T, preferred_element_type=jnp.float32).astype(jnp.bfloat16)
     rows_grad = lax.all_gather(own_grad, "grp", axis=0, tiled=True)
-    weight_grad = lax.psum(local_grad, ("grp", "row")) * (1.0 / math.sqrt(verts))
+    weight_grad = lax.psum(lax.psum(local_grad, "grp"), "row") * (1.0 / math.sqrt(verts))
     by_block = rows_grad.reshape(-1, block, width)
 
     def spread(carry, items):

time: 746 us -> 1140 us (1.53)
  waiting for transfers between devices: 542 us -> 931 us
    psum x1 -> x2, waiting for transfers between devices: 58.5 us -> 447 us  [the longest x1 427 us: body(): lax.psum(lax.psum(local_grad, 'grp'), 'row') * (1.0 / math.sqrt(verts))]
  transfers between devices with their start and end apart: 4 -> 5, of which waited for: 4 -> 5; matrix products, arithmetic and copies ran while one was open for 11% -> 7% of each run, Pallas kernels for 0% -> 0%
where the time goes in v1:
time: 1140 us; the launch traced here: 1130 us
  waiting for transfers between devices  931 us (82%)
  local copies, waits for them, and re-layouts  83.4 us (7%)
  other arithmetic  62 us (5%)
  matrix products  32.9 us (3%)
  between operations  13.8 us (1%)
    psum x1, waiting for transfers between devices, body(): lax.psum(lax.psum(local_grad, 'grp'), 'row') * (1.0 / math.sqrt(verts))  427 us
    reduce_scatter x1, waiting for transfers between devices, body(): lax.psum_scatter(term, 'row', scatter_dimension=0, tiled=True)  339 us
    all_gather x1, waiting for transfers between devices, body(): gathered = lax.all_gather(features, 'row', axis=0, tiled=True)  127 us
    gather x8, local copies, waits for them, and re-layouts, aggregate(): picked = panel_blocks[columns]  51.1 us
    scatter-add x8, other arithmetic, spread(): return (carry.at[columns].add(contrib), None)  36.9 us
  transfers between devices with their start and end apart: 5, of which 5 were waited for; matrix products, arithmetic and copies ran while one was open for 7% of the time, Pallas kernels for 0%

profile of v1, /device:TPU:0, one launch (start us, length us, event | category | flops | bytes accessed | tf_op | source)
XLA Modules:
  0.0 1133.8 jit_solution(7264399422172430454)
XLA Ops:
  8.0 127.3 %all-gather.2.cloned.1.call-done = bf16[32768,256]{1,0:T(8,128)(2,1)} async-done(((bf16[512,256]{1,0:T(8,128)(2,1)}), bf16[32768,256]{1,0:T(8,128)(2,1)}) %all-gather.2.cloned.1.call-update) | async-done | bytes 16777232 | tf_op jit(solution)/shard_map/all_gather | solution.py:21
  135.3 88.4 %while.22 = (s32[]{:T(128)}, f32[8,128,256]{2,1,0:T(8,128)}, s32[8]{0:T(128)}, bf16[8,16,128,128]{3,2,1,0:T(8,128)(2,1)}, s32[8,16]{1,0:T(8,128)}, /*index=5*/bf16[256,128,256]{2,1,0:T(8,128)(2,1)}, s32[]{:T(128)}) while((s32[]{:T(128)}, f32[8,128,256]{2,1,0:T(8,128)}, s32[8]{0:T(128)}, bf16[8,16,128,128]{3,2,1,0:T(8,128)(2,1)}, ...), condition=%wide.region_1.2_spmd.clone, body=%wide.region_0.1_spmd.clone.sunk | while | flops 134480960 | bytes 3806601 | solution.py:31
  135.3 1.2 dynamic_slice.67
  137.9 6.4 gather_fusion
  144.3 2.1 fusion.42
  146.3 1.2 dynamic_slice.67
  148.9 6.4 gather_fusion
  155.3 2.1 fusion.42
  160.0 6.4 gather_fusion
  166.4 2.1 fusion.42
  171.0 6.4 gather_fusion
  177.4 2.1 fusion.42
  182.1 6.4 gather_fusion
  188.5 2.0 fusion.42
  193.1 6.4 gather_fusion
  199.5 2.1 fusion.42
  204.1 6.4 gather_fusion
  210.5 2.1 fusion.42
  215.2 6.4 gather_fusion
  221.6 2.0 fusion.42
  223.7 6.5 copy.9
  230.2 17.2 %reduce-scatter.3.cloned.1.call-done = f32[512,256]{1,0:T(8,128)} async-done(((f32[1024,256]{1,0:T(8,128)}), f32[512,256]{1,0:T(8,128)}) %reduce-scatter.3.cloned.1.call-update) | async-done | bytes 524304 | tf_op jit(solution)/shard_map/reduce_scatter | solution.py:34
  247.4 2.1 multiply_convert_fusion
  249.5 2.0 fusion.24
  251.9 10.2 all_gather.7
  262.1 20.3 %all-reduce.3.cloned.1.call-done = f32[256,256]{1,0:T(8,128)} async-done(((f32[256,256]{1,0:T(8,128)}), f32[256,256]{1,0:T(8,128)}) %all-reduce.3.cloned.1.call-update) | async-done | bytes 262160 | tf_op jit(solution)/shard_map/psum | solution.py:42
  282.5 11.2 broadcast_in_dim.28
  293.7 64.6 %while.23 = (s32[]{:T(128)}, f32[256,128,256]{2,1,0:T(8,128)}, s32[8,16]{1,0:T(8,128)}, s32[8]{0:T(128)S(1)}, bf16[8,16,128,128]{2,3,1,0:T(8,128)(2,1)}, /*index=5*/bf16[8,128,256]{2,1,0:T(8,128)(2,1)S(1)}, s32[]{:T(128)}) while((s32[]{:T(128)}, f32[256,128,256]{2,1,0:T(8,128)}, s32[8,16]{1,0:T(8,128)}, s32[8]{0:T(128)S(1)}, ...), condition=%wide.region_7.8_spmd.clone, body=%wide.region_5.7_spmd.clone.sunk | while | flops 135004224 | bytes 8980281 | solution.py:51
  295.7 1.5 fusion.46
  297.2 4.6 scatter_fusion
  303.8 1.5 fusion.46
  305.3 4.6 scatter_fusion
  311.8 1.5 fusion.46
  313.4 4.6 scatter_fusion
  319.9 1.5 fusion.46
  321.4 4.6 scatter_fusion
  328.0 1.5 fusion.46
  329.5 4.6 scatter_fusion
  336.0 1.5 fusion.46
  337.6 4.6 scatter_fusion
  344.1 1.5 fusion.46
  345.6 4.6 scatter_fusion
  352.2 1.5 fusion.46
  353.7 4.6 scatter_fusion
  358.3 426.9 %all-reduce.5.cloned.1.call-done = f32[256,256]{1,0:T(8,128)} async-done(((f32[256,256]{1,0:T(8,128)}), f32[256,256]{1,0:T(8,128)}) %all-reduce.5.cloned.1.call-update) | async-done | bytes 262160 | tf_op jit(solution)/shard_map/psum | solution.py:42
  785.2 1.7 broadcast_multiply_fusion
  786.9 338.6 %reduce-scatter.5.cloned.1.call-done = f32[512,256]{1,0:T(8,128)} async-done(((f32[32768,256]{1,0:T(8,128)}), f32[512,256]{1,0:T(8,128)}) %reduce-scatter.5.cloned.1.call-update) | async-done | bytes 524304 | tf_op jit(solution)/shard_map/reduce_scatter | solution.py:57
  1125.5 1.8 convert_element_type.23
  (74 shorter events, 35.0 us)
Async XLA Ops:
  7.2 240.2 %copy-start = (bf16[256,256]{1,0:T(8,128)(2,1)S(1)}, bf16[256,256]{1,0:T(8,128)(2,1)}, u32[]{:S(2)}) copy-start(bf16[256,256]{1,0:T(8,128)(2,1)} %param.11) | copy-start | bytes 393220
  7.2 128.1 %all-gather.2.cloned.1.call-start = ((), (), s32[]{:S(2)}) async-start(), calls=%async_computation.2 | async-start | bytes 17039360 | tf_op jit(solution)/shard_map/all_gather | solution.py:21
  7.9 239.5 %reduce-scatter.3.cloned.1.call-start = ((), (), s32[]{:S(2)}) async-start(), calls=%async_computation.3 | async-start | bytes 1572864 | tf_op jit(solution)/shard_map/reduce_scatter | solution.py:34
  223.7 23.7 %copy-start.2 = (bf16[512,256]{1,0:T(8,128)(2,1)S(1)}, bf16[512,256]{1,0:T(8,128)(2,1)}, u32[]{:S(2)}) copy-start(bf16[512,256]{1,0:T(8,128)(2,1)} %param.15) | copy-start | bytes 786436
  223.7 58.7 %all-reduce.3.cloned.1.call-start = ((), (), s32[]{:S(2)}) async-start(), calls=%async_computation.4 | async-start | bytes 524288 | tf_op jit(solution)/shard_map/psum | solution.py:42
  251.6 533.7 %all-reduce.5.cloned.1.call-start = ((), (), s32[]{:S(2)}) async-start(), calls=%async_computation.5 | async-start | bytes 524288 | tf_op jit(solution)/shard_map/psum | solution.py:42
  282.4 843.1 %reduce-scatter.5.cloned.1.call-start = ((), (), s32[]{:S(2)}) async-start(), calls=%async_computation.6 | async-start | bytes 34078720 | tf_op jit(solution)/shard_map/reduce_scatter | solution.py:57
  282.5 11.3 copy-start.3
  358.3 769.0 %copy-start.1 = (bf16[256,256]{1,0:T(8,128)(2,1)S(1)}, bf16[256,256]{1,0:T(8,128)(2,1)}, u32[]{:S(2)}) copy-start(bf16[256,256]{1,0:T(8,128)(2,1)} %param.11) | copy-start | bytes 393220
Sparse Core Ops, SparseCore 0:
  9.7 125.4 all-gather.1
  223.8 23.5 reduce-scatter.2
  251.7 30.6 all-reduce.2
  284.7 500.4 all-reduce.4
  787.6 337.8 reduce-scatter.4
